TPU v7x, 32 devices: a whole 2x2x4 slice. The times are simulated.
32 devices in a mesh: ctx: 8 (over z, y), seq: 4 (over x, core).
Axes of the slice: x: 2, y: 2, z: 4, core: 2. Of those that a mesh axis runs over, the one named last changes fastest.
Arguments:
- tokens: bfloat16 [16384, 1024], P(('ctx', 'seq')), may hold values from -60 to 60
- w_qkv: bfloat16 [1024, 3072], replicated, may hold values from -1 to 1
- w_out: bfloat16 [1024, 1024], replicated, may hold values from -0.1875 to 0.1875
- counts: int32 [256], replicated, may hold values from 1 to 64
- rand_seg: int32 [256, 3], replicated, may hold values from 0 to 7, all different within a row; in each aligned block of 8 rows (0 to 7, 8 to 15, ...) at most 4 rows name the same one
- rand_off: int32 [256, 3], replicated, may hold values from 0 to 7
Outputs:
- mixed: bfloat16 [16384, 1024], P(('ctx', 'seq'))
Inputs may be any that keep to these rules, and one draw needn't show every extreme that they name: `rand_seg`: each row names 3 different segments; among the 8 rows of one device no segment is named more than 4 times, a bound that some block reaches.
All inputs are finite; a program needn't handle non-finite values.
Results may differ from a plain program's by a relative error of at most 0.0045.
The roundings to bfloat16 on the way count: a program that leaves them out, or rounds other values in their place, can miss the bound.
Values may be sent and summed in bfloat16 or wider, within the bound.
No kernel may reach another device: no remote copies, remote signals or barrier semaphores. Data moves between devices by JAX's collectives and lax.ppermute only.
A program may use at most 192 MiB of HBM per device.

v0:
```python
import math
import jax
import jax.numpy as jnp
from jax import lax
from jax.sharding import PartitionSpec as P

HD = 64
BLK = 64
RAND = 3
G_DEV = 8


def with_halo(block, sides, width):
    for axis, dim in sides:
        count = lax.axis_size(axis)
        forward = [(i, i + 1) for i in range(count - 1)]
        backward = [(target, source) for source, target in forward]
        low = lax.ppermute(
            lax.slice_in_dim(block, block.shape[dim] - width, None, axis=dim), axis, forward
        )
        high = lax.ppermute(lax.slice_in_dim(block, 0, width, axis=dim), axis, backward)
        block = jnp.concatenate([low, block, high], axis=dim)
    return block


def for_sending(x):

    def short(part):
        return part.astype(jnp.bfloat16) if part.dtype == jnp.float32 else part

    return jax.tree.map(short, x)


def attend(queries, nearby, distant, global_k, global_v, block_ids, far_ids, counts):
    span, block_len, head_count, head_dim = queries.shape
    width = head_count * head_dim
    block_total = counts.shape[0]
    scaling = 1.0 / math.sqrt(head_dim)
    key_parts = []
    value_parts = []
    part_counts = []
    for offset in range(3):
        piece = nearby[offset : offset + span]
        near_ids = block_ids + (offset - 1)
        existing = (near_ids >= 0) & (near_ids < block_total)
        part_counts.append(
            jnp.where(existing, jnp.take(counts, jnp.clip(near_ids, 0, block_total - 1)), 0)
        )
        key_parts.append(piece[..., :width].reshape(span, block_len, head_count, head_dim))
        value_parts.append(piece[..., width:].reshape(span, block_len, head_count, head_dim))
    for index in range(distant.shape[1]):
        piece = distant[:, index]
        part_counts.append(jnp.take(counts, far_ids[:, index]))
        key_parts.append(piece[..., :width].reshape(span, block_len, head_count, head_dim))
        value_parts.append(piece[..., width:].reshape(span, block_len, head_count, head_dim))
    positions = jnp.arange(block_len, dtype=jnp.int32)[None, None, None, :]
    score_parts = []
    for keys_now, count_now in zip(key_parts, part_counts):
        scores = (
            jnp.einsum("bqhd,bkhd->bhqk", queries, keys_now, preferred_element_type=jnp.float32)
            * scaling
        )
        score_parts.append(jnp.where(positions < count_now[:, None, None, None], scores, -jnp.inf))
    wide_scores = (
        jnp.einsum("bqhd,khd->bhqk", queries, global_k, preferred_element_type=jnp.float32)
        * scaling
    )
    peak_score = jnp.max(wide_scores, axis=-1)
    for scores in score_parts:
        peak_score = jnp.maximum(peak_score, jnp.max(scores, axis=-1))
    peak_score = peak_score[..., None]
    wide_exp = jnp.exp(wide_scores - peak_score)
    denominator = jnp.sum(wide_exp, axis=-1, keepdims=True)
    exp_parts = []
    for scores in score_parts:
        exps = jnp.exp(scores - peak_score)
        denominator = denominator + jnp.sum(exps, axis=-1, keepdims=True)
        exp_parts.append(exps)
    wide_prob = (wide_exp / denominator).astype(jnp.bfloat16)
    result = jnp.einsum("bhqk,khd->bqhd", wide_prob, global_v, preferred_element_type=jnp.float32)
    for exps, values_now in zip(exp_parts, value_parts):
        probs = (exps / denominator).astype(jnp.bfloat16)
        result = result + jnp.einsum(
            "bhqk,bkhd->bqhd", probs, values_now, preferred_element_type=jnp.float32
        )
    return result.astype(jnp.bfloat16)


def positions_among(owners, owner_count):
    marks = (owners[..., None] == jnp.arange(owner_count, dtype=jnp.int32)).astype(jnp.int32)
    ranks = jnp.cumsum(marks, axis=-2) - 1
    return jnp.sum(ranks * marks, axis=-1)


def serve_slots(owners, offsets, target, capacity):
    matched = owners == target
    ranks = jnp.cumsum(matched.astype(jnp.int32), axis=-1) - 1
    slot_hit = matched[..., None, :] & (
        ranks[..., None, :] == jnp.arange(capacity, dtype=jnp.int32)[:, None]
    )
    return jnp.sum(jnp.where(slot_hit, offsets[..., None, :], 0), axis=-1)


def run_groups(
    queries, near_blocks, distant, far_global, global_k, global_v, first_id, span, counts
):
    block_count = queries.shape[0]

    def one_group(start):
        group_queries = lax.dynamic_slice_in_dim(queries, start, span, 0)
        nearby = lax.dynamic_slice_in_dim(near_blocks, start, span + 2, 0)
        distant_part = lax.dynamic_slice_in_dim(distant, start, span, 0)
        far_ids = lax.dynamic_slice_in_dim(far_global, start, span, 0)
        block_ids = first_id + start + jnp.arange(span, dtype=jnp.int32)
        return attend(
            group_queries, nearby, distant_part, global_k, global_v, block_ids, far_ids, counts
        )

    starts = jnp.arange(block_count // span, dtype=jnp.int32) * span
    outputs = lax.map(one_group, starts)
    return outputs.reshape(block_count * queries.shape[1], -1)


def regroup(w_qkv, groups, head_total):
    model_dim = w_qkv.shape[0]
    shaped = w_qkv.reshape(model_dim, groups, head_total // groups, 3, HD)
    return jnp.transpose(shaped, (0, 1, 3, 2, 4)).reshape(model_dim, 3 * model_dim)


def local(tokens, w_qkv, w_out, counts, rand_seg, rand_off):
    seq_count = lax.axis_size("seq")
    ctx_count = lax.axis_size("ctx")
    seq_index = lax.axis_index("seq")
    ctx_index = lax.axis_index("ctx")
    tok_rows, model_dim = tokens.shape
    head_total = model_dim // HD
    head_local = head_total // seq_count
    seg_rows = tok_rows * seq_count
    seg_blocks = seg_rows // BLK
    dev_blocks = tok_rows // BLK
    local_width = head_local * HD
    capacity = (RAND * dev_blocks + ctx_count - 1) // ctx_count + 1
    first_block = (ctx_index * seq_count + seq_index) * dev_blocks
    own_counts = lax.dynamic_slice_in_dim(counts, first_block, dev_blocks)
    usable = (jnp.arange(BLK, dtype=jnp.int32)[None, :] < own_counts[:, None]).reshape(tok_rows)
    group_rows = tok_rows // G_DEV
    member = (
        jnp.arange(tok_rows, dtype=jnp.int32)[None, :] // group_rows
        == jnp.arange(G_DEV, dtype=jnp.int32)[:, None]
    )
    pooling = (member & usable[None, :]).astype(jnp.bfloat16)
    sums = jnp.dot(pooling, tokens, preferred_element_type=jnp.float32)
    pooled = sums / jnp.sum(pooling.astype(jnp.float32), axis=1, keepdims=True)
    summary = (pooled / jnp.sqrt(jnp.mean(pooled * pooled, axis=1, keepdims=True) + 1e-05)).astype(
        jnp.bfloat16
    )
    w_summary = w_qkv.reshape(model_dim, head_total, 3, HD)[:, :, 1:, :].reshape(
        model_dim, 2 * model_dim
    )
    summary_kv = jnp.dot(summary, w_summary, preferred_element_type=jnp.float32).astype(
        jnp.bfloat16
    )
    every_head = lax.all_gather(summary_kv, ("ctx", "seq"), axis=0, tiled=True)
    summary_heads = every_head.reshape(-1, head_total, 2, HD)
    all_owner = rand_seg.reshape(ctx_count, seq_count, dev_blocks * RAND)
    all_offset = rand_off.reshape(ctx_count, seq_count, dev_blocks * RAND)
    w_ordered = regroup(w_qkv, seq_count, head_total)
    qkv = jnp.dot(tokens, w_ordered, preferred_element_type=jnp.float32).astype(jnp.bfloat16)
    seg_qkv = lax.all_to_all(qkv, "seq", split_axis=1, concat_axis=0, tiled=True)
    my_heads = lax.dynamic_slice_in_dim(summary_heads, seq_index * head_local, head_local, 1)
    global_k = my_heads[:, :, 0, :]
    global_v = my_heads[:, :, 1, :]
    queries = seg_qkv[:, :local_width].reshape(seg_blocks, BLK, head_local, HD)
    own_kv = seg_qkv[:, local_width:]
    kv_cols = 2 * local_width
    rimmed = with_halo(own_kv, (("ctx", 0),), BLK)
    near_blocks = rimmed.reshape(seg_blocks + 2, BLK, kv_cols)
    seg_first = ctx_index * seg_blocks
    my_owner = lax.dynamic_slice_in_dim(rand_seg, seg_first, seg_blocks)
    my_offset = lax.dynamic_slice_in_dim(rand_off, seg_first, seg_blocks)
    block_rows = own_kv.reshape(seg_blocks, BLK * kv_cols)
    send_off = serve_slots(all_owner, all_offset, ctx_index, capacity)
    send_ids = send_off + (jnp.arange(seq_count, dtype=jnp.int32) * dev_blocks)[None, :, None]
    outgoing = jnp.take(block_rows, send_ids.reshape(-1), axis=0).reshape(
        ctx_count, seq_count * capacity, BLK * kv_cols
    )
    incoming = lax.all_to_all(outgoing, "ctx", split_axis=0, concat_axis=0, tiled=True)
    mine = my_owner.reshape(seq_count, dev_blocks * RAND)
    slot_ids = (
        mine * (seq_count * capacity)
        + jnp.arange(seq_count, dtype=jnp.int32)[:, None] * capacity
        + positions_among(mine, ctx_count)
    )
    fetched = jnp.take(
        incoming.reshape(ctx_count * seq_count * capacity, BLK * kv_cols),
        slot_ids.reshape(-1),
        axis=0,
    )
    distant = fetched.reshape(seg_blocks, RAND, BLK, kv_cols)
    slot_of_row = jnp.arange(seg_blocks, dtype=jnp.int32) // dev_blocks
    far_global = my_owner * seg_blocks + (slot_of_row * dev_blocks)[:, None] + my_offset
    attended = run_groups(
        queries, near_blocks, distant, far_global, global_k, global_v, seg_first, 8, counts
    )
    returned = lax.all_to_all(
        for_sending(attended), "seq", split_axis=0, concat_axis=1, tiled=True
    ).astype(attended.dtype)
    mixed = tokens.astype(jnp.float32) + jnp.dot(
        returned, w_out, preferred_element_type=jnp.float32
    )
    return mixed.astype(jnp.bfloat16)


def solution(mesh):
    in_specs = (P(("ctx", "seq"), None), P(), P(), P(), P(), P())
    out_specs = P(("ctx", "seq"), None)
    return jax.shard_map(local, mesh=mesh, in_specs=in_specs, out_specs=out_specs, check_vma=False)
```

profile of v0, /device:TPU:0, one launch (start us, length us, event | category | flops | bytes accessed | tf_op | source)
XLA Modules:
  0.0 729.9 jit_solution(17863630455531703478)
XLA Ops:
  6.5 8.8 %copy.355 = bf16[1024,3072]{0,1:T(8,128)(2,1)} copy(bf16[1024,3072]{1,0:T(8,128)(2,1)} %param.11) | data formatting | bytes 12582912 | tf_op args[1]
  15.4 3.6 copy.356
  19.0 3.7 convolution_convert_fusion
  24.6 4.8 all-to-all-start
  31.7 35.4 %all-to-all-done = bf16[512,4,768]{2,0,1:T(8,128)(2,1)} async-done(((bf16[512,4,768]{2,0,1:T(8,128)(2,1)}), bf16[512,4,768]{2,0,1:T(8,128)(2,1)}, u32[]{:S(2)}, u32[]{:S(2)}) %all-to-all-start) | async-done | bytes 3145760 | tf_op jit(solution)/shard_map/all_to_all | solution.py:169
  70.1 4.5 reshape.469
  74.5 31.8 %gather_fusion.6 = bf16[128,32768]{1,0:T(8,128)(2,1)} fusion(bf16[32,32768]{1,0:T(8,128)(2,1)} %reshape.469, s32[1024]{0:T(1024)S(1)} %pad_clamp_fusion.7), kind=kCustom, calls=%fused_computation.6 | custom fusion | bytes 16777728 | tf_op jit(solution)/shard_map/jit(_take)/gather | solution.py:184
  106.3 7.5 %broadcast_select_fusion = bf16[8,16,32768]{2,1,0:T(8,128)(2,1)} fusion(bf16[8,16,32768]{2,1,0:T(8,128)(2,1)} %bitcast.152, pred[8,16]{1,0:T(8,128)(4,1)S(1)} %compare_and_fusion), kind=kLoop, calls=%fused_computation.141 | loop fusion | flops 4194304 | bytes 16777344 | tf_op jit(solution)/shard_map/jit(_take)/select_n | solution.py:184
  113.8 6.6 all-to-all-start.1
  120.5 4.9 slice.116
  126.1 4.0 convolution_convert_fusion.1
  131.7 191.1 %all-gather.2.cloned.1.call-done = bf16[256,2048]{1,0:T(8,128)(2,1)} async-done(((bf16[8,2048]{1,0:T(8,128)(2,1)}), bf16[256,2048]{1,0:T(8,128)(2,1)}) %all-gather.2.cloned.1.call-update) | async-done | bytes 1048592 | tf_op jit(solution)/shard_map/all_gather | solution.py:163
  326.5 4.5 collective-permute-start
  338.0 17.1 %gather_fusion.7 = bf16[96,32768]{1,0:T(8,128)(2,1)} fusion(bf16[128,32768]{1,0:T(8,128)(2,1)} %bitcast.34, s32[1024]{0:T(1024)S(1)} %pad_clamp_fusion.6), kind=kCustom, calls=%fused_computation.7 | custom fusion | bytes 12583296 | tf_op jit(solution)/shard_map/jit(_take)/gather | solution.py:194
  355.1 5.3 copy.401
  363.7 335.4 %while.10 = (s32[]{:T(128)}, bf16[4,8,64,4,64]{2,1,4,3,0:T(8,128)(2,1)}, s32[4]{0:T(128)S(1)}, bf16[32,64,4,64]{3,2,1,0:T(4,128)(2,1)}, bf16[256,4,64]{0,2,1:T(8...) while((s32[]{:T(128)}, ...), condition=%wide.region_21.23_spmd, body=%wide.region_6.22_spmd.sunk | while | flops 347477696 | bytes 71337048 | solution.py:120
  396.2 3.3 fusion.129
  417.0 3.3 fusion.134
  480.0 3.3 fusion.129
  500.8 3.3 fusion.134
  563.7 3.3 fusion.129
  647.5 3.3 fusion.129
  702.3 16.9 %all_to_all.43 = bf16[4,512,256]{1,2,0:T(8,128)(2,1)S(1)} all-to-all(bf16[4,512,256]{1,2,0:T(8,128)(2,1)S(1)} %all_to_all.36), channel_id=1, replica_groups=mesh['ctx'=8,'seq'=4] {'seq'}, dimensions={0} | all-to-all | bytes 2097152 | tf_op jit(solution)/shard_map/all_to_all | solution.py:205
  719.2 3.5 add_convert_fusion
  (491 shorter events, 325.9 us)
Async XLA Ops:
  6.5 712.7 %copy-start = (bf16[1024,1024]{1,0:T(8,128)(2,1)S(1)}, bf16[1024,1024]{1,0:T(8,128)(2,1)}, u32[]{:S(2)}) copy-start(bf16[1024,1024]{1,0:T(8,128)(2,1)} %param.12) | copy-start | bytes 6291460
  24.6 4.8 copy-start.22
  24.6 5.1 copy-start.21
  24.6 42.5 %all-to-all-start = ((bf16[512,4,768]{2,0,1:T(8,128)(2,1)}), bf16[512,4,768]{2,0,1:T(8,128)(2,1)}, u32[]{:S(2)}, u32[]{:S(2)}) async-start(bf16[512,4,768]{2,0,1:T(8,128)(2,1)} %bitcast.156), calls=%async_computation | async-start | bytes 6291456 | tf_op jit(solution)/shard_map/all_to_all | solution.py:169
  30.7 43.8 %copy-start.23 = (s32[4]{0:T(128)}, s32[4]{0:T(128)S(1)}, u32[]{:S(2)}) copy-start(s32[4]{0:T(128)S(1)} %iota_multiply_fusion.1) | copy-start | bytes 52
  113.8 224.2 %all-to-all-start.1 = ((bf16[8,16,32768]{2,1,0:T(8,128)(2,1)}), bf16[8,16,32768]{2,1,0:T(8,128)(2,1)}, u32[]{:S(2)}, u32[]{:S(2)}) async-start(bf16[8,16,32768]{2,1,0:T(8,128)(2,1)} %broadcast_select_fusion), calls=%async_computation.1 | async-start | bytes 16777216 | tf_op jit(solution)/shard_map/all_to_all | solution.py:187
  120.4 202.5 %all-gather.2.cloned.1.call-start = ((), (), s32[]{:S(2)}) async-start(), calls=%async_computation.3 | async-start | bytes 1081344 | tf_op jit(solution)/shard_map/all_gather | solution.py:163
  120.4 5.0 copy-start.1
  325.2 9.7 %collective-permute-start.1 = (bf16[64,512]{1,0:T(8,128)(2,1)S(1)}, bf16[64,512]{1,0:T(8,128)(2,1)S(1)}, u32[]{:S(2)}, u32[]{:S(2)}) collective-permute-start(bf16[64,512]{1,0:T(8,128)(2,1)S(1)} %get-tuple-element.218), channel_id=1, source_target_pairs={{4,0},{8,4},{12,8},{16,12},{20,16},{24,20},{28,24},{5,1},{9,5},{13... | collective-permute-start | bytes 196616 | tf_op jit(solution)/shard_map/ppermute | solution.py:21
  326.5 8.4 %collective-permute-start = (bf16[64,512]{1,0:T(8,128)(2,1)S(1)}, bf16[64,512]{1,0:T(8,128)(2,1)S(1)}, u32[]{:S(2)}, u32[]{:S(2)}) collective-permute-start(bf16[64,512]{1,0:T(8,128)(2,1)S(1)} %get-tuple-element.217), channel_id=1, source_target_pairs={{0,4},{4,8},{8,12},{12,16},{16,20},{20,24},{24,28},{1,5},{5,9},{9,... | collective-permute-start | bytes 196616 | tf_op jit(solution)/shard_map/ppermute | solution.py:18
  396.1 6.2 copy-start.20
  400.2 7.4 %copy-start.19 = (s32[8]{0:T(128)S(1)}, s32[8]{0:T(128)}, u32[]{:S(2)}) copy-start(s32[8]{0:T(128)} %get-tuple-element.360) | copy-start | bytes 100 | tf_op jit(solution)/shard_map/while
  425.5 4.0 copy-start.9
  440.0 4.6 copy-start.10
  479.9 6.2 copy-start.20
  484.0 7.4 %copy-start.19 = (s32[8]{0:T(128)S(1)}, s32[8]{0:T(128)}, u32[]{:S(2)}) copy-start(s32[8]{0:T(128)} %get-tuple-element.360) | copy-start | bytes 100 | tf_op jit(solution)/shard_map/while
  509.2 4.0 copy-start.9
  523.8 4.6 copy-start.10
  563.6 6.2 copy-start.20
  567.8 7.4 %copy-start.19 = (s32[8]{0:T(128)S(1)}, s32[8]{0:T(128)}, u32[]{:S(2)}) copy-start(s32[8]{0:T(128)} %get-tuple-element.360) | copy-start | bytes 100 | tf_op jit(solution)/shard_map/while
  607.6 4.6 copy-start.10
  647.4 6.2 copy-start.20
  651.5 7.4 %copy-start.19 = (s32[8]{0:T(128)S(1)}, s32[8]{0:T(128)}, u32[]{:S(2)}) copy-start(s32[8]{0:T(128)} %get-tuple-element.360) | copy-start | bytes 100 | tf_op jit(solution)/shard_map/while
  691.3 4.6 copy-start.10
  (64 other events, 137.1 us)
Sparse Core Ops, SparseCore 0:
  130.3 192.5 all-gather.1
where the time goes:
time: 737 us; the launch traced here: 730 us
  local copies, waits for them, and re-layouts  229 us (31%)
  waiting for transfers between devices  227 us (31%)
  matrix products  149 us (20%)
  other arithmetic  61.5 us (8%)
  starting transfers between devices  17.3 us (2%)
  blocking collectives  16.9 us (2%)
  loops' own time  16 us (2%)
  between operations  14.1 us (2%)
    all_gather x1, waiting for transfers between devices, local(): every_head = lax.all_gather(summary_kv, ('ctx', 'seq'), axis=0, tiled=True)  191 us
    dot_general x24, matrix products, attend(): jnp.einsum('bqhd,bkhd->bhqk', queries, keys_now, preferred_element_type=j...  67.6 us
    dot_general x24, matrix products, attend(): jnp.einsum('bhqk,bkhd->bqhd', probs, values_now, preferred_element_type=j...  53.1 us
    reshape x24, local copies, waits for them, and re-layouts, attend(): piece[..., :width].reshape(span, block_len, head_count, head_dim)  41.3 us
    all_to_all x1, waiting for transfers between devices, local(): lax.all_to_all(qkv, 'seq', split_axis=1, concat_axis=0, tiled=True)  35.4 us
    gather x1, local copies, waits for them, and re-layouts, local(): jnp.take(block_rows, send_ids.reshape(-1), axis=0)  31.8 us
    reshape x24, local copies, waits for them, and re-layouts, attend(): piece[..., width:].reshape(span, block_len, head_count, head_dim)  31.4 us
    gather x1, local copies, waits for them, and re-layouts, local(): jnp.take(incoming.reshape(ctx_count * seq_count * capacity, BLK * kv_cols...  17.1 us
  transfers between devices with their start and end apart: 5, of which 2 were waited for; matrix products, arithmetic and copies ran while one was open for 3% of the time, Pallas kernels for 0%

commit v1 on v0

--- a/solution.py
+++ b/solution.py
@@ -166,7 +166,9 @@
     all_offset = rand_off.reshape(ctx_count, seq_count, dev_blocks * RAND)
     w_ordered = regroup(w_qkv, seq_count, head_total)
     qkv = jnp.dot(tokens, w_ordered, preferred_element_type=jnp.float32).astype(jnp.bfloat16)
-    seg_qkv = lax.all_to_all(qkv, "seq", split_axis=1, concat_axis=0, tiled=True)
+    seg_qkv = jnp.concatenate(
+        lax.all_to_all(jnp.stack(jnp.split(qkv, lax.axis_size("seq"), axis=1)), "seq", 0, 0), axis=0
+    )
     my_heads = lax.dynamic_slice_in_dim(summary_heads, seq_index * head_local, head_local, 1)
     global_k = my_heads[:, :, 0, :]
     global_v = my_heads[:, :, 1, :]

time: 737 us -> 744 us (level)
  no operation moved by 1% of the time
where the time goes in v1:
time: 744 us; the launch traced here: 736 us
  local copies, waits for them, and re-layouts  231 us (31%)
  waiting for transfers between devices  227 us (31%)
  matrix products  149 us (20%)
  other arithmetic  66.7 us (9%)
  starting transfers between devices  17.3 us (2%)
  blocking collectives  16.9 us (2%)
  loops' own time  15.7 us (2%)
  between operations  14.1 us (2%)
    all_gather x1, waiting for transfers between devices, local(): every_head = lax.all_gather(summary_kv, ('ctx', 'seq'), axis=0, tiled=True)  191 us
    dot_general x24, matrix products, attend(): jnp.einsum('bqhd,bkhd->bhqk', queries, keys_now, preferred_element_type=j...  67.4 us
    dot_general x24, matrix products, attend(): jnp.einsum('bhqk,bkhd->bqhd', probs, values_now, preferred_element_type=j...  53.3 us
    reshape x24, local copies, waits for them, and re-layouts, attend(): piece[..., :width].reshape(span, block_len, head_count, head_dim)  41.3 us
    all_to_all x1, waiting for transfers between devices, local(): lax.all_to_all(jnp.stack(jnp.split(qkv, lax.axis_size('seq'), axis=1)), '...  35.4 us
    gather x1, local copies, waits for them, and re-layouts, local(): jnp.take(block_rows, send_ids.reshape(-1), axis=0)  31.8 us
    reshape x24, local copies, waits for them, and re-layouts, attend(): piece[..., width:].reshape(span, block_len, head_count, head_dim)  31.2 us
    slice x12, local copies, waits for them, and re-layouts, attend(): piece[..., width:].reshape(span, block_len, head_count, head_dim)  20.7 us
  transfers between devices with their start and end apart: 5, of which 2 were waited for; matrix products, arithmetic and copies ran while one was open for 3% of the time, Pallas kernels for 0%

profile of v1, /device:TPU:0, one launch (start us, length us, event | category | flops | bytes accessed | tf_op | source)
XLA Modules:
  0.0 736.3 jit_solution(13135037306395041357)
XLA Ops:
  6.5 8.8 %copy.350 = bf16[1024,3072]{0,1:T(8,128)(2,1)} copy(bf16[1024,3072]{1,0:T(8,128)(2,1)} %param.11) | data formatting | bytes 12582912 | tf_op args[1]
  15.4 3.6 copy.351
  19.0 3.7 convolution_convert_fusion
  24.8 4.8 all-to-all-start
  31.9 35.4 %all-to-all-done = bf16[4,512,768]{2,1,0:T(8,128)(2,1)} async-done(((bf16[4,512,768]{2,1,0:T(8,128)(2,1)}), bf16[4,512,768]{2,1,0:T(8,128)(2,1)}, u32[]{:S(2)}, u32[]{:S(2)}) %all-to-all-start) | async-done | bytes 3145760 | tf_op jit(solution)/shard_map/all_to_all | solution.py:170
  70.3 4.5 reshape.470
  74.8 31.8 %gather_fusion.6 = bf16[128,32768]{1,0:T(8,128)(2,1)} fusion(bf16[32,32768]{1,0:T(8,128)(2,1)} %reshape.470, s32[1024]{0:T(1024)S(1)} %pad_clamp_fusion.7), kind=kCustom, calls=%fused_computation.6 | custom fusion | bytes 16777728 | tf_op jit(solution)/shard_map/jit(_take)/gather | solution.py:186
  106.6 7.5 %broadcast_select_fusion = bf16[8,16,32768]{2,1,0:T(8,128)(2,1)} fusion(bf16[8,16,32768]{2,1,0:T(8,128)(2,1)} %bitcast.154, pred[8,16]{1,0:T(8,128)(4,1)S(1)} %compare_and_fusion), kind=kLoop, calls=%fused_computation.141 | loop fusion | flops 4194304 | bytes 16777344 | tf_op jit(solution)/shard_map/jit(_take)/select_n | solution.py:186
  114.0 6.6 all-to-all-start.1
  120.7 4.9 slice.116
  126.4 4.0 convolution_convert_fusion.1
  131.9 191.1 %all-gather.2.cloned.1.call-done = bf16[256,2048]{1,0:T(8,128)(2,1)} async-done(((bf16[8,2048]{1,0:T(8,128)(2,1)}), bf16[256,2048]{1,0:T(8,128)(2,1)}) %all-gather.2.cloned.1.call-update) | async-done | bytes 1048592 | tf_op jit(solution)/shard_map/all_gather | solution.py:163
  326.7 4.5 collective-permute-start
  338.3 17.1 %gather_fusion.7 = bf16[96,32768]{1,0:T(8,128)(2,1)} fusion(bf16[128,32768]{1,0:T(8,128)(2,1)} %bitcast.36, s32[1024]{0:T(1024)S(1)} %pad_clamp_fusion.6), kind=kCustom, calls=%fused_computation.7 | custom fusion | bytes 12583296 | tf_op jit(solution)/shard_map/jit(_take)/gather | solution.py:196
  355.3 5.3 copy.394
  360.6 3.3 copy_select_fusion
  363.9 341.6 %while.10 = (s32[]{:T(128)}, bf16[4,8,64,4,64]{2,1,4,3,0:T(8,128)(2,1)}, s32[4]{0:T(128)S(1)}, bf16[32,64,4,64]{3,2,1,0:T(4,128)(2,1)}, bf16[256,4,64]{0,2,1:T(8...) while((s32[]{:T(128)}, ...), condition=%wide.region_21.23_spmd, body=%wide.region_6.22_spmd.sunk | while | flops 347477696 | bytes 69043080 | solution.py:120
  396.4 3.3 fusion.129
  418.8 3.3 fusion.134
  504.2 3.3 fusion.134
  589.5 3.3 fusion.134
  674.8 3.3 fusion.134
  708.7 16.9 %all_to_all.29 = bf16[4,512,256]{1,2,0:T(8,128)(2,1)S(1)} all-to-all(bf16[4,512,256]{1,2,0:T(8,128)(2,1)S(1)} %all_to_all.22), channel_id=1, replica_groups=mesh['ctx'=8,'seq'=4] {'seq'}, dimensions={0} | all-to-all | bytes 2097152 | tf_op jit(solution)/shard_map/all_to_all | solution.py:207
  725.6 3.5 add_convert_fusion
  (436 shorter events, 332.8 us)
Async XLA Ops:
  6.5 719.1 %copy-start = (bf16[1024,1024]{1,0:T(8,128)(2,1)S(1)}, bf16[1024,1024]{1,0:T(8,128)(2,1)}, u32[]{:S(2)}) copy-start(bf16[1024,1024]{1,0:T(8,128)(2,1)} %param.12) | copy-start | bytes 6291460
  24.8 4.8 copy-start.15
  24.8 5.1 copy-start.14
  24.8 42.5 %all-to-all-start = ((bf16[4,512,768]{2,1,0:T(8,128)(2,1)}), bf16[4,512,768]{2,1,0:T(8,128)(2,1)}, u32[]{:S(2)}, u32[]{:S(2)}) async-start(bf16[4,512,768]{2,1,0:T(8,128)(2,1)} %pad_maximum_fusion), calls=%async_computation | async-start | bytes 6291456 | tf_op jit(solution)/shard_map/all_to_all | solution.py:170
  31.0 43.8 %copy-start.16 = (s32[4]{0:T(128)}, s32[4]{0:T(128)S(1)}, u32[]{:S(2)}) copy-start(s32[4]{0:T(128)S(1)} %iota_multiply_fusion.1) | copy-start | bytes 52
  114.0 224.2 %all-to-all-start.1 = ((bf16[8,16,32768]{2,1,0:T(8,128)(2,1)}), bf16[8,16,32768]{2,1,0:T(8,128)(2,1)}, u32[]{:S(2)}, u32[]{:S(2)}) async-start(bf16[8,16,32768]{2,1,0:T(8,128)(2,1)} %broadcast_select_fusion), calls=%async_computation.1 | async-start | bytes 16777216 | tf_op jit(solution)/shard_map/all_to_all | solution.py:189
  120.6 202.5 %all-gather.2.cloned.1.call-start = ((), (), s32[]{:S(2)}) async-start(), calls=%async_computation.3 | async-start | bytes 1081344 | tf_op jit(solution)/shard_map/all_gather | solution.py:163
  120.7 5.0 copy-start.1
  325.4 9.7 %collective-permute-start.1 = (bf16[64,512]{1,0:T(8,128)(2,1)S(1)}, bf16[64,512]{1,0:T(8,128)(2,1)S(1)}, u32[]{:S(2)}, u32[]{:S(2)}) collective-permute-start(bf16[64,512]{1,0:T(8,128)(2,1)S(1)} %get-tuple-element.218), channel_id=1, source_target_pairs={{4,0},{8,4},{12,8},{16,12},{20,16},{24,20},{28,24},{5,1},{9,5},{13... | collective-permute-start | bytes 196616 | tf_op jit(solution)/shard_map/ppermute | solution.py:21
  326.7 8.4 %collective-permute-start = (bf16[64,512]{1,0:T(8,128)(2,1)S(1)}, bf16[64,512]{1,0:T(8,128)(2,1)S(1)}, u32[]{:S(2)}, u32[]{:S(2)}) collective-permute-start(bf16[64,512]{1,0:T(8,128)(2,1)S(1)} %get-tuple-element.217), channel_id=1, source_target_pairs={{0,4},{4,8},{8,12},{12,16},{16,20},{20,24},{24,28},{1,5},{5,9},{9,... | collective-permute-start | bytes 196616 | tf_op jit(solution)/shard_map/ppermute | solution.py:18
  392.1 11.4 %copy-start.13 = (s32[8]{0:T(128)S(1)}, s32[8]{0:T(128)}, u32[]{:S(2)}) copy-start(s32[8]{0:T(128)} %get-tuple-element.361) | copy-start | bytes 100 | tf_op jit(solution)/shard_map/while
  396.4 12.4 %copy-start.12 = (s32[8]{0:T(128)S(1)}, s32[8]{0:T(128)}, u32[]{:S(2)}) copy-start(s32[8]{0:T(128)} %get-tuple-element.364) | copy-start | bytes 100 | tf_op jit(solution)/shard_map/while
  418.8 4.1 copy-start.11
  439.9 6.5 copy-start.9
  477.4 11.4 %copy-start.13 = (s32[8]{0:T(128)S(1)}, s32[8]{0:T(128)}, u32[]{:S(2)}) copy-start(s32[8]{0:T(128)} %get-tuple-element.361) | copy-start | bytes 100 | tf_op jit(solution)/shard_map/while
  481.7 12.4 %copy-start.12 = (s32[8]{0:T(128)S(1)}, s32[8]{0:T(128)}, u32[]{:S(2)}) copy-start(s32[8]{0:T(128)} %get-tuple-element.364) | copy-start | bytes 100 | tf_op jit(solution)/shard_map/while
  525.3 6.5 copy-start.9
  562.7 11.4 %copy-start.13 = (s32[8]{0:T(128)S(1)}, s32[8]{0:T(128)}, u32[]{:S(2)}) copy-start(s32[8]{0:T(128)} %get-tuple-element.361) | copy-start | bytes 100 | tf_op jit(solution)/shard_map/while
  567.0 12.4 %copy-start.12 = (s32[8]{0:T(128)S(1)}, s32[8]{0:T(128)}, u32[]{:S(2)}) copy-start(s32[8]{0:T(128)} %get-tuple-element.364) | copy-start | bytes 100 | tf_op jit(solution)/shard_map/while
  589.5 4.1 copy-start.11
  610.6 6.5 copy-start.9
  648.0 11.4 %copy-start.13 = (s32[8]{0:T(128)S(1)}, s32[8]{0:T(128)}, u32[]{:S(2)}) copy-start(s32[8]{0:T(128)} %get-tuple-element.361) | copy-start | bytes 100 | tf_op jit(solution)/shard_map/while
  652.3 12.4 %copy-start.12 = (s32[8]{0:T(128)S(1)}, s32[8]{0:T(128)}, u32[]{:S(2)}) copy-start(s32[8]{0:T(128)} %get-tuple-element.364) | copy-start | bytes 100 | tf_op jit(solution)/shard_map/while
  695.9 6.5 copy-start.9
  (36 other events, 96.5 us)
Sparse Core Ops, SparseCore 0:
  130.5 192.5 all-gather.1
